TPU v7x, 32 devices: a whole 2x2x4 slice. The times are simulated.
32 devices in a mesh: req: 16 (over z, x, core), ep: 2 (over y).
Axes of the slice: x: 2, y: 2, z: 4, core: 2. Of those that a mesh axis runs over, the one named last changes fastest.
Arguments:
- hidden: bfloat16 [16, 512, 1536], P('req', None, 'ep'), may hold values from -6 to 6
- key_cache: bfloat16 [16, 8, 2560, 64], P('req', 'ep'), may hold values from -160 to 160
- value_cache: bfloat16 [16, 8, 2560, 64], P('req', 'ep'), may hold values from -6 to 6
- request_order: int32 [16], replicated, may hold values from 0 to 15, each once
- cached_lengths: int32 [16], replicated, may hold values from 1 to 2048, 16384 in all
- expert_ids: int32 [16, 512, 8], P('req'), may hold values from 0 to 39, all different within a row; in each aligned block of 512 rows (0 to 511, 512 to 1023, ..., all dimensions but the last counted through in order) at most 192 rows name the same one
- gate_values: float32 [16, 512, 8], P('req'), may hold values from 0.1 to 1
- attn_gain: float32 [1536], replicated, may hold values from 0.25 to 1.75
- ffn_gain: float32 [1536], replicated, may hold values from 0.25 to 1.75
- w_query: bfloat16 [1536, 1536], P(None, 'ep'), may hold values from -0.15625 to 0.15625
- w_key: bfloat16 [1536, 512], P(None, 'ep'), may hold values from -0.15625 to 0.15625
- w_value: bfloat16 [1536, 512], P(None, 'ep'), may hold values from -0.15625 to 0.15625
- w_out: bfloat16 [1536, 1536], P('ep'), may hold values from -0.15625 to 0.15625
- expert_gate: bfloat16 [4, 1536, 512], P('ep', 'req'), may hold values from -0.15625 to 0.15625
- expert_up: bfloat16 [4, 1536, 512], P('ep', 'req'), may hold values from -0.15625 to 0.15625
- expert_down: bfloat16 [4, 512, 1536], P('ep', 'req'), may hold values from -0.25 to 0.25
Outputs:
- hidden_out: bfloat16 [16, 512, 1536], P('req', None, 'ep')
- key_cache_out: bfloat16 [16, 8, 2560, 64], P('req', 'ep')
- value_cache_out: bfloat16 [16, 8, 2560, 64], P('req', 'ep')
Inputs may be any that keep to these rules, and one draw needn't show every extreme that they name: Slot s holds request request_order[s]; every request is held by one slot. `cached_lengths`: the longest cached length is exactly 2048. `expert_ids`: each token names 8 different experts; among the 512 tokens of one slot no expert is named by more than 192 tokens, a bound that some block reaches.
All inputs are finite; a program needn't handle non-finite values.
Results may differ from a plain program's by a relative error of at most 0.012.
The roundings to bfloat16 on the way count: a program that leaves them out, or rounds other values in their place, can miss the bound.
Values may be sent and summed in bfloat16 or wider, within the bound.
No kernel may reach another device: no remote copies, remote signals or barrier semaphores. Data moves between devices by JAX's collectives and lax.ppermute only.
A program may use at most 128 MiB of HBM per device.

v0:
```python
import jax
import jax.numpy as jnp
from jax import lax
from jax.sharding import PartitionSpec as P

epsilon = 1e-06


def normalize(values, gain):
    return values * lax.rsqrt(jnp.mean(values * values, -1, keepdims=True) + epsilon) * gain


def rotate(values, positions):
    half = values.shape[-1] // 2
    freq = 10000.0 ** (-jnp.arange(half, dtype=jnp.float32) * (2.0 / values.shape[-1]))
    angle = positions.astype(jnp.float32)[:, None] * freq[None, :]
    cosine = jnp.cos(angle)
    sine = jnp.sin(angle)
    first = values[..., :half]
    second = values[..., half:]
    return jnp.concatenate([first * cosine - second * sine, second * cosine + first * sine], -1)


def rounded(values):
    return lax.optimization_barrier(values.astype(jnp.bfloat16)).astype(jnp.float32)


def route_tables(chosen, gate_rows, wanted, capacity):
    hits = chosen[:, :, None] == wanted[None, None, :]
    member = jnp.sum(hits.astype(jnp.int32), 1, dtype=jnp.int32)
    weight = jnp.sum(jnp.where(hits, gate_rows[:, :, None], 0.0), 1)
    place = jnp.cumsum(member, 0, dtype=jnp.int32) - 1
    slots = jnp.arange(capacity, dtype=jnp.int32)
    table = (member.T[:, None, :] == 1) & (place.T[:, None, :] == slots[None, :, None])
    gate_slot = jnp.sum(jnp.where(table, weight.T[:, None, :], 0.0), 2)
    return (table.astype(jnp.bfloat16), gate_slot)


def attend(query, keys, values, length, new_rows):
    query_rows = query.shape[1]
    blocks = keys.shape[1] // new_rows
    limit = length + jnp.arange(query_rows, dtype=jnp.int32) % new_rows
    scale = query.shape[2] ** (-0.5)

    def visit(carry, block):
        running, total, summed = carry
        start = block * new_rows
        key_block = lax.dynamic_slice_in_dim(keys, start, new_rows, 1)
        value_block = lax.dynamic_slice_in_dim(values, start, new_rows, 1)
        scores = (
            jnp.einsum("kqd,kjd->kqj", query, key_block, preferred_element_type=jnp.float32) * scale
        )
        column = start + jnp.arange(new_rows, dtype=jnp.int32)
        visible = column[None, :] <= limit[:, None]
        scores = jnp.where(visible[None], scores, -1e30)
        highest = jnp.maximum(running, jnp.max(scores, -1))
        correction = jnp.exp(running - highest)
        probs = jnp.where(visible[None], jnp.exp(scores - highest[..., None]), 0.0)
        total = total * correction + jnp.sum(probs, -1)
        summed = summed * correction[..., None] + jnp.einsum(
            "kqj,kjd->kqd",
            probs.astype(jnp.bfloat16),
            value_block,
            preferred_element_type=jnp.float32,
        )
        return ((highest, total, summed), None)

    start_state = (
        jnp.full(query.shape[:2], -1e30, jnp.float32),
        jnp.zeros(query.shape[:2], jnp.float32),
        jnp.zeros(query.shape, jnp.float32),
    )
    final, unused = lax.scan(visit, start_state, jnp.arange(blocks, dtype=jnp.int32))
    return final[2] / final[1][..., None]


def on_device(
    hidden,
    key_cache,
    value_cache,
    request_order,
    cached_lengths,
    expert_ids,
    gate_values,
    attn_gain,
    ffn_gain,
    w_query,
    w_key,
    w_value,
    w_out,
    expert_gate,
    expert_up,
    expert_down,
):
    own_rows = hidden[0]
    new_rows = own_rows.shape[0]
    own_width = own_rows.shape[1]
    head_dim = key_cache.shape[3]
    kv_local = key_cache.shape[1]
    heads_local = w_query.shape[1] // head_dim
    group = heads_local // kv_local
    per_device = expert_gate.shape[0]
    devices = lax.axis_size("ep")
    capacity = 3 * new_rows // 8
    everyone = jnp.arange(request_order.shape[0], dtype=jnp.int32)
    request = jnp.sum(jnp.where(everyone == lax.axis_index("req"), request_order, 0))
    length = jnp.sum(jnp.where(everyone == request, cached_lengths, 0))
    rows_whole = lax.all_gather(own_rows, "ep", axis=1, tiled=True)
    width = rows_whole.shape[1]
    normed = normalize(rows_whole.astype(jnp.float32), attn_gain).astype(jnp.bfloat16)
    query = jnp.dot(normed, w_query, preferred_element_type=jnp.float32)
    key_new = jnp.dot(normed, w_key, preferred_element_type=jnp.float32)
    value_new = jnp.dot(normed, w_value, preferred_element_type=jnp.float32)
    positions = length + jnp.arange(new_rows, dtype=jnp.int32)
    query = rotate(
        query.reshape(new_rows, heads_local, head_dim).transpose(1, 0, 2), positions
    ).astype(jnp.bfloat16)
    query = query.reshape(kv_local, group * new_rows, head_dim)
    key_new = rotate(
        key_new.reshape(new_rows, kv_local, head_dim).transpose(1, 0, 2), positions
    ).astype(jnp.bfloat16)
    value_new = (
        value_new.reshape(new_rows, kv_local, head_dim).transpose(1, 0, 2).astype(jnp.bfloat16)
    )
    zero = jnp.zeros((), jnp.int32)
    keys = lax.dynamic_update_slice(key_cache[0], key_new, (zero, length, zero))
    values = lax.dynamic_update_slice(value_cache[0], value_new, (zero, length, zero))
    attended = attend(query, keys, values, length, new_rows)
    attended = (
        attended.reshape(heads_local, new_rows, head_dim)
        .transpose(1, 0, 2)
        .reshape(new_rows, heads_local * head_dim)
        .astype(jnp.bfloat16)
    )
    partial_value = rounded(jnp.dot(attended, w_out, preferred_element_type=jnp.float32))
    head_sum = lax.psum_scatter(
        partial_value.astype(jnp.bfloat16), "ep", scatter_dimension=1, tiled=True
    ).astype(jnp.float32)
    mixed = (own_rows.astype(jnp.float32) + head_sum).astype(jnp.bfloat16)
    mixed_f = mixed.astype(jnp.float32)
    chosen = expert_ids[0]
    gate_rows = gate_values[0]
    first = lax.axis_index("ep") * per_device
    squares = jnp.sum(mixed_f * mixed_f, -1)
    totals = lax.psum(squares, "ep")
    local_gain = lax.dynamic_slice_in_dim(ffn_gain, lax.axis_index("ep") * own_width, own_width)
    normed_cols = (mixed_f * lax.rsqrt(totals / width + epsilon)[:, None] * local_gain).astype(
        jnp.bfloat16
    )
    table_all, gate_all = route_tables(
        chosen, gate_rows, jnp.arange(per_device * devices, dtype=jnp.int32), capacity
    )
    buffers = jnp.einsum(
        "ect,td->ecd", table_all, normed_cols, preferred_element_type=jnp.float32
    ).astype(jnp.bfloat16)
    inputs = lax.all_to_all(buffers, "ep", split_axis=0, concat_axis=2, tiled=True)
    gate_own = lax.dynamic_slice_in_dim(gate_all, first, per_device, 0)
    columns = inputs
    gate_next = jnp.einsum(
        "ecd,edf->ecf",
        columns,
        lax.all_gather(expert_gate, "req", axis=1, tiled=True),
        preferred_element_type=jnp.float32,
    )
    up_next = jnp.einsum(
        "ecd,edf->ecf",
        columns,
        lax.all_gather(expert_up, "req", axis=1, tiled=True),
        preferred_element_type=jnp.float32,
    )
    hidden_act = (jax.nn.silu(gate_next) * up_next).astype(jnp.bfloat16)
    columns = hidden_act
    output = jnp.einsum(
        "ecf,efd->ecd",
        columns,
        lax.all_gather(expert_down, "req", axis=1, tiled=True),
        preferred_element_type=jnp.float32,
    )
    contrib = (output * gate_own[..., None]).astype(jnp.bfloat16)
    returned = lax.all_to_all(contrib, "ep", split_axis=2, concat_axis=0, tiled=True)
    per_expert = jnp.einsum("ect,ecd->etd", table_all, returned, preferred_element_type=jnp.float32)
    grouped = rounded(jnp.sum(per_expert.reshape(devices, per_device, new_rows, own_width), 1))
    expert_sum = jnp.sum(grouped, 0)
    result = (mixed_f + expert_sum).astype(jnp.bfloat16)
    return (result[None], keys[None], values[None])


def solution(mesh):
    in_specs = (
        P("req", None, "ep"),
        P("req", "ep", None, None),
        P("req", "ep", None, None),
        P(),
        P(),
        P("req", None, None),
        P("req", None, None),
        P(),
        P(),
        P(None, "ep"),
        P(None, "ep"),
        P(None, "ep"),
        P("ep", None),
        P("ep", "req", None),
        P("ep", "req", None),
        P("ep", "req", None),
    )
    out_specs = (P("req", None, "ep"), P("req", "ep", None, None), P("req", "ep", None, None))
    return jax.shard_map(
        on_device, mesh=mesh, in_specs=in_specs, out_specs=out_specs, check_vma=False
    )
```

profile of v0, /device:TPU:0, one launch (start us, length us, event | category | flops | bytes accessed | tf_op | source)
XLA Modules:
  0.0 390.4 jit_solution(1194642636352865639)
XLA Ops:
  8.1 2.6 copy.81
  16.7 25.2 %all-gather.12.cloned.1.call-done = bf16[1,512,1536]{2,1,0:T(8,128)(2,1)} async-done(((bf16[1,512,768]{2,1,0:T(8,128)(2,1)}), bf16[1,512,1536]{2,1,0:T(8,128)(2,1)}) %all-gather.12.cloned.1.call-update) | async-done | bytes 1572880 | tf_op jit(solution)/shard_map/all_gather | solution.py:108
  54.8 4.0 %dynamic_update_slice.6 = bf16[4,2560,64]{1,2,0:T(8,128)(2,1)} dynamic-update-slice(bf16[4,2560,64]{1,2,0:T(8,128)(2,1)} %bitcast.102, bf16[4,512,64]{1,2,0:T(8,128)(2,1)S(1)} %pad_maximum_fusion.1, s32[]{:T(128)} %constant.31.clone.1, s32[]{:T(128)S(6)} %select_n.46, s32[]{:T(128)} %constant.31.clone.1) | dynamic-update-slice | bytes 524292 | tf_op jit(solution)/shard_map/dynamic_update_slice | solution.py:126
  61.1 3.8 dynamic_update_slice.7
  64.9 123.9 %while.15 = (s32[]{:T(128)}, f32[4,1536]{1,0:T(4,128)S(1)}, f32[4,1536]{1,0:T(4,128)S(1)}, f32[4,1536,64]{1,2,0:T(8,128)}, s32[5]{0:T(128)S(1)}, /*index=5*/bf16...) while((s32[]{:T(128)}, f32[4,1536]{1,0:T(4,128)S(1)}, ...), condition=%wide.region_6.7_spmd.clone, body=%wide.region_3.6_spmd.clone.sunk | while | flops 848208896 | bytes 96092400 | solution.py:73
  67.5 8.1 %fusion.93 = (f32[4,1536]{1,0:T(4,128)S(1)}, f32[4,512,1536]{2,1,0:T(8,128)}) fusion(pred[1536,512]{0,1:T(8,128)(4,1)S(1)} %broadcast_compare_fusion.3, bf16[4,1536,64]{1,2,0:T(8,128)(2,1)} %get-tuple-element.236, bf16[4,2560,64]{1,2,0:T(8,128)(2,1)} %get-tuple-element.235, s32[]{:T(128)S(6)} %select_n.102), kind=kOutput, calls=%fused_computation.3.clone.1 | convolution fusion | flops 412084224 | bytes 14442500 | tf_op jit(solution)/shard_map/while/body/eval_jaxpr/kqd,kjd->kqj/dot_general | solution.py:51
  75.6 6.9 %fusion.94 = f32[4,1536]{1,0:T(4,128)S(1)} fusion(f32[4,512,1536]{2,1,0:T(8,128)} %get-tuple-element.201, f32[4,1536]{1,0:T(4,128)S(1)} %select_maximum_fusion.2, pred[1536,512]{0,1:T(8,128)(4,1)S(1)} %broadcast_compare_fusion.3), kind=kLoop, calls=%fused_computation.5.clone.1 | loop fusion | flops 15722496 | bytes 13418496 | tf_op jit(solution)/shard_map/while/body/eval_jaxpr/reduce_sum | solution.py:59
  83.8 5.7 %fusion.96 = f32[4,1536,64]{1,2,0:T(8,128)} fusion(f32[4,512,1536]{2,1,0:T(8,128)S(1)} %copy-done.1, f32[4,1536]{1,0:T(4,128)S(1)} %select_maximum_fusion.2, pred[1536,512]{0,1:T(8,128)(4,1)S(1)} %broadcast_compare_fusion.3, f32[4,1536,64]{1,2,0:T(8,128)} %get-tuple-element.220, f32[4,1536]{1,0:T(4,128)S(1)} %get-tuple-element.203, pred[]{:T(512)S(6)} %compare.4, ...), kind=kOutput, calls=%fused_computation.8.clone.1 | convolution fusion | flops 419561472 | bytes 16826372 | tf_op jit(solution)/shard_map/while/body/eval_jaxpr/kqj,kjd->kqd/dot_general | solution.py:60
  92.1 8.1 %fusion.93 = (f32[4,1536]{1,0:T(4,128)S(1)}, f32[4,512,1536]{2,1,0:T(8,128)}) fusion(pred[1536,512]{0,1:T(8,128)(4,1)S(1)} %broadcast_compare_fusion.3, bf16[4,1536,64]{1,2,0:T(8,128)(2,1)} %get-tuple-element.236, bf16[4,2560,64]{1,2,0:T(8,128)(2,1)} %get-tuple-element.235, s32[]{:T(128)S(6)} %select_n.102), kind=kOutput, calls=%fused_computation.3.clone.1 | convolution fusion | flops 412084224 | bytes 14442500 | tf_op jit(solution)/shard_map/while/body/eval_jaxpr/kqd,kjd->kqj/dot_general | solution.py:51
  100.1 6.9 %fusion.94 = f32[4,1536]{1,0:T(4,128)S(1)} fusion(f32[4,512,1536]{2,1,0:T(8,128)} %get-tuple-element.201, f32[4,1536]{1,0:T(4,128)S(1)} %select_maximum_fusion.2, pred[1536,512]{0,1:T(8,128)(4,1)S(1)} %broadcast_compare_fusion.3), kind=kLoop, calls=%fused_computation.5.clone.1 | loop fusion | flops 15722496 | bytes 13418496 | tf_op jit(solution)/shard_map/while/body/eval_jaxpr/reduce_sum | solution.py:59
  108.4 6.0 %fusion.96 = f32[4,1536,64]{1,2,0:T(8,128)} fusion(f32[4,512,1536]{2,1,0:T(8,128)S(1)} %copy-done.1, f32[4,1536]{1,0:T(4,128)S(1)} %select_maximum_fusion.2, pred[1536,512]{0,1:T(8,128)(4,1)S(1)} %broadcast_compare_fusion.3, f32[4,1536,64]{1,2,0:T(8,128)} %get-tuple-element.220, f32[4,1536]{1,0:T(4,128)S(1)} %get-tuple-element.203, pred[]{:T(512)S(6)} %compare.4, ...), kind=kOutput, calls=%fused_computation.8.clone.1 | convolution fusion | flops 419561472 | bytes 16826372 | tf_op jit(solution)/shard_map/while/body/eval_jaxpr/kqj,kjd->kqd/dot_general | solution.py:60
  116.9 8.1 %fusion.93 = (f32[4,1536]{1,0:T(4,128)S(1)}, f32[4,512,1536]{2,1,0:T(8,128)}) fusion(pred[1536,512]{0,1:T(8,128)(4,1)S(1)} %broadcast_compare_fusion.3, bf16[4,1536,64]{1,2,0:T(8,128)(2,1)} %get-tuple-element.236, bf16[4,2560,64]{1,2,0:T(8,128)(2,1)} %get-tuple-element.235, s32[]{:T(128)S(6)} %select_n.102), kind=kOutput, calls=%fused_computation.3.clone.1 | convolution fusion | flops 412084224 | bytes 14442500 | tf_op jit(solution)/shard_map/while/body/eval_jaxpr/kqd,kjd->kqj/dot_general | solution.py:51
  125.0 6.9 %fusion.94 = f32[4,1536]{1,0:T(4,128)S(1)} fusion(f32[4,512,1536]{2,1,0:T(8,128)} %get-tuple-element.201, f32[4,1536]{1,0:T(4,128)S(1)} %select_maximum_fusion.2, pred[1536,512]{0,1:T(8,128)(4,1)S(1)} %broadcast_compare_fusion.3), kind=kLoop, calls=%fused_computation.5.clone.1 | loop fusion | flops 15722496 | bytes 13418496 | tf_op jit(solution)/shard_map/while/body/eval_jaxpr/reduce_sum | solution.py:59
  133.2 6.0 %fusion.96 = f32[4,1536,64]{1,2,0:T(8,128)} fusion(f32[4,512,1536]{2,1,0:T(8,128)S(1)} %copy-done.1, f32[4,1536]{1,0:T(4,128)S(1)} %select_maximum_fusion.2, pred[1536,512]{0,1:T(8,128)(4,1)S(1)} %broadcast_compare_fusion.3, f32[4,1536,64]{1,2,0:T(8,128)} %get-tuple-element.220, f32[4,1536]{1,0:T(4,128)S(1)} %get-tuple-element.203, pred[]{:T(512)S(6)} %compare.4, ...), kind=kOutput, calls=%fused_computation.8.clone.1 | convolution fusion | flops 419561472 | bytes 16826372 | tf_op jit(solution)/shard_map/while/body/eval_jaxpr/kqj,kjd->kqd/dot_general | solution.py:60
  141.7 8.1 %fusion.93 = (f32[4,1536]{1,0:T(4,128)S(1)}, f32[4,512,1536]{2,1,0:T(8,128)}) fusion(pred[1536,512]{0,1:T(8,128)(4,1)S(1)} %broadcast_compare_fusion.3, bf16[4,1536,64]{1,2,0:T(8,128)(2,1)} %get-tuple-element.236, bf16[4,2560,64]{1,2,0:T(8,128)(2,1)} %get-tuple-element.235, s32[]{:T(128)S(6)} %select_n.102), kind=kOutput, calls=%fused_computation.3.clone.1 | convolution fusion | flops 412084224 | bytes 14442500 | tf_op jit(solution)/shard_map/while/body/eval_jaxpr/kqd,kjd->kqj/dot_general | solution.py:51
  149.8 6.9 %fusion.94 = f32[4,1536]{1,0:T(4,128)S(1)} fusion(f32[4,512,1536]{2,1,0:T(8,128)} %get-tuple-element.201, f32[4,1536]{1,0:T(4,128)S(1)} %select_maximum_fusion.2, pred[1536,512]{0,1:T(8,128)(4,1)S(1)} %broadcast_compare_fusion.3), kind=kLoop, calls=%fused_computation.5.clone.1 | loop fusion | flops 15722496 | bytes 13418496 | tf_op jit(solution)/shard_map/while/body/eval_jaxpr/reduce_sum | solution.py:59
  158.1 6.0 %fusion.96 = f32[4,1536,64]{1,2,0:T(8,128)} fusion(f32[4,512,1536]{2,1,0:T(8,128)S(1)} %copy-done.1, f32[4,1536]{1,0:T(4,128)S(1)} %select_maximum_fusion.2, pred[1536,512]{0,1:T(8,128)(4,1)S(1)} %broadcast_compare_fusion.3, f32[4,1536,64]{1,2,0:T(8,128)} %get-tuple-element.220, f32[4,1536]{1,0:T(4,128)S(1)} %get-tuple-element.203, pred[]{:T(512)S(6)} %compare.4, ...), kind=kOutput, calls=%fused_computation.8.clone.1 | convolution fusion | flops 419561472 | bytes 16826372 | tf_op jit(solution)/shard_map/while/body/eval_jaxpr/kqj,kjd->kqd/dot_general | solution.py:60
  166.6 8.1 %fusion.93 = (f32[4,1536]{1,0:T(4,128)S(1)}, f32[4,512,1536]{2,1,0:T(8,128)}) fusion(pred[1536,512]{0,1:T(8,128)(4,1)S(1)} %broadcast_compare_fusion.3, bf16[4,1536,64]{1,2,0:T(8,128)(2,1)} %get-tuple-element.236, bf16[4,2560,64]{1,2,0:T(8,128)(2,1)} %get-tuple-element.235, s32[]{:T(128)S(6)} %select_n.102), kind=kOutput, calls=%fused_computation.3.clone.1 | convolution fusion | flops 412084224 | bytes 14442500 | tf_op jit(solution)/shard_map/while/body/eval_jaxpr/kqd,kjd->kqj/dot_general | solution.py:51
  174.7 6.9 %fusion.94 = f32[4,1536]{1,0:T(4,128)S(1)} fusion(f32[4,512,1536]{2,1,0:T(8,128)} %get-tuple-element.201, f32[4,1536]{1,0:T(4,128)S(1)} %select_maximum_fusion.2, pred[1536,512]{0,1:T(8,128)(4,1)S(1)} %broadcast_compare_fusion.3), kind=kLoop, calls=%fused_computation.5.clone.1 | loop fusion | flops 15722496 | bytes 13418496 | tf_op jit(solution)/shard_map/while/body/eval_jaxpr/reduce_sum | solution.py:59
  182.9 6.0 %fusion.96 = f32[4,1536,64]{1,2,0:T(8,128)} fusion(f32[4,512,1536]{2,1,0:T(8,128)S(1)} %copy-done.1, f32[4,1536]{1,0:T(4,128)S(1)} %select_maximum_fusion.2, pred[1536,512]{0,1:T(8,128)(4,1)S(1)} %broadcast_compare_fusion.3, f32[4,1536,64]{1,2,0:T(8,128)} %get-tuple-element.220, f32[4,1536]{1,0:T(4,128)S(1)} %get-tuple-element.203, pred[]{:T(512)S(6)} %compare.4, ...), kind=kOutput, calls=%fused_computation.8.clone.1 | convolution fusion | flops 419561472 | bytes 16826372 | tf_op jit(solution)/shard_map/while/body/eval_jaxpr/kqj,kjd->kqd/dot_general | solution.py:60
  200.4 22.6 %reduce-scatter.2.cloned.1.call-done = bf16[512,768]{1,0:T(8,128)(2,1)} async-done(((bf16[512,1536]{1,0:T(8,128)(2,1)}), bf16[512,768]{1,0:T(8,128)(2,1)}) %reduce-scatter.2.cloned.1.call-update) | async-done | bytes 786448 | tf_op jit(solution)/shard_map/reduce_scatter | solution.py:136
  224.5 5.2 %psum.7 = f32[512]{0:T(512)S(1)} all-reduce(f32[512]{0:T(512)S(1)} %fusion.28), channel_id=1, replica_groups=mesh['req'=16,'ep'=2] {'ep'}, use_global_device_ids=true, to_apply=%region_12.13 | all-reduce | flops 512 | bytes 4096 | tf_op jit(solution)/shard_map/psum | solution.py:145
  229.7 3.2 fusion.40
  232.9 4.6 %all-to-all-start = ((bf16[4,192,768]{2,1,0:T(8,128)(2,1)}), bf16[4,192,768]{2,1,0:T(8,128)(2,1)}, u32[]{:S(2)}, u32[]{:S(2)}) async-start(bf16[4,192,768]{2,1,0:T(8,128)(2,1)} %fusion.40), calls=%async_computation.1 | async-start | bytes 2359296 | tf_op jit(solution)/shard_map/all_to_all | solution.py:156
  238.0 14.2 %all-to-all-done = bf16[4,192,768]{2,1,0:T(8,128)(2,1)} async-done(((bf16[4,192,768]{2,1,0:T(8,128)(2,1)}), bf16[4,192,768]{2,1,0:T(8,128)(2,1)}, u32[]{:S(2)}, u32[]{:S(2)}) %all-to-all-start) | async-done | bytes 1179680 | tf_op jit(solution)/shard_map/all_to_all | solution.py:156
  254.6 3.9 %fusion.68 = f32[2,192,512]{2,1,0:T(8,128)} fusion(bf16[2,192,1536]{2,1,0:T(8,128)(2,1)} %bitcast.104, bf16[2,1536,512]{2,1,0:T(8,128)(2,1)} %all-gather.6.cloned.1.call-done), kind=kOutput, calls=%fused_computation.100 | convolution fusion | flops 603979776 | bytes 5111808 | tf_op jit(solution)/shard_map/ecd,edf->ecf/dot_general | solution.py:159
  258.5 32.5 %all-gather.10.cloned.1.call-done = bf16[2,512,1536]{2,1,0:T(8,128)(2,1)} async-done(((bf16[2,32,1536]{2,1,0:T(8,128)(2,1)}), bf16[2,512,1536]{2,1,0:T(8,128)(2,1)}) %all-gather.10.cloned.1.call-update) | async-done | bytes 3145744 | tf_op jit(solution)/shard_map/all_gather | solution.py:176
  291.0 46.1 %all-gather.8.cloned.1.call-done = bf16[2,1536,512]{2,1,0:T(8,128)(2,1)} async-done(((bf16[2,96,512]{2,1,0:T(8,128)(2,1)}), bf16[2,1536,512]{2,1,0:T(8,128)(2,1)}) %all-gather.8.cloned.1.call-update) | async-done | bytes 3145744 | tf_op jit(solution)/shard_map/all_gather | solution.py:168
  337.2 5.9 %fusion.27 = bf16[2,192,1536]{2,1,0:T(8,128)(2,1)} fusion(bf16[2,512,1536]{2,1,0:T(8,128)(2,1)} %all-gather.10.cloned.1.call-done, f32[2,192]{1,0:T(2,128)S(1)} %constant_dynamic-slice_fusion, bf16[2,192,1536]{2,1,0:T(8,128)(2,1)} %bitcast.105, bf16[2,1536,512]{2,1,0:T(8,128)(2,1)} %all-gather.8.cloned.1.call-done, f32[2,192,512]{2,1,0:T(8,128)} %fusion.68), kind=kOutput, calls=%fused_computation.39 | convolution fusion | flops 1210318848 | bytes 9438720 | tf_op jit(solution)/shard_map/ecf,efd->ecd/dot_general | solution.py:173
  343.1 4.8 %copy.57 = bf16[2,192,1536]{1,0,2:T(2,128)(2,1)} copy(bf16[2,192,1536]{2,1,0:T(8,128)(2,1)} %fusion.27) | data formatting | bytes 2359296 | tf_op jit(solution)/shard_map/convert_element_type | solution.py:179
  347.9 25.2 %all_to_all.36 = bf16[2,192,1536]{1,0,2:T(2,128)(2,1)} all-to-all(bf16[2,192,1536]{1,0,2:T(2,128)(2,1)} %copy.57), channel_id=1, replica_groups=mesh['req'=16,'ep'=2] {'ep'}, dimensions={2} | all-to-all | bytes 2359296 | tf_op jit(solution)/shard_map/all_to_all | solution.py:180
  373.1 4.9 %copy.58 = bf16[2,192,2,768]{3,1,0,2:T(8,128)(2,1)} copy(bf16[2,192,2,768]{1,0,3,2:T(2,128)(2,1)} %bitcast.101) | data formatting | bytes 2359296 | tf_op jit(solution)/shard_map/all_to_all | solution.py:180
  (127 shorter events, 56.0 us)
Async XLA Ops:
  8.0 186.2 %copy-start = (bf16[768,1536]{1,0:T(8,128)(2,1)S(1)}, bf16[768,1536]{1,0:T(8,128)(2,1)}, u32[]{:S(2)}) copy-start(bf16[768,1536]{1,0:T(8,128)(2,1)} %param.30) | copy-start | bytes 7077892
  8.0 33.8 %all-gather.12.cloned.1.call-start = ((), (), s32[]{:S(2)}) async-start(), calls=%async_computation.7 | async-start | bytes 2359296 | tf_op jit(solution)/shard_map/all_gather | solution.py:108
  8.1 2.6 copy-start.5
  10.7 1.2 copy-start.11
  10.7 1.8 copy-start.12
  11.8 32.0 %copy-start.10 = (f32[1536]{0:T(1024)S(1)}, f32[1536]{0:T(1024)}, u32[]{:S(2)}) copy-start(f32[1536]{0:T(1024)} %param.25) | copy-start | bytes 18436
  11.8 211.3 %reduce-scatter.2.cloned.1.call-start = ((), (), s32[]{:S(2)}) async-start(), calls=%async_computation.3 | async-start | bytes 2359296 | tf_op jit(solution)/shard_map/reduce_scatter | solution.py:136
  41.8 1.9 copy-start.4
  43.8 2.2 copy-start.9
  75.6 8.3 %copy-start.1 = (f32[4,512,1536]{2,1,0:T(8,128)S(1)}, f32[4,512,1536]{2,1,0:T(8,128)}, u32[]{:S(2)}) copy-start(f32[4,512,1536]{2,1,0:T(8,128)} %get-tuple-element.201) | copy-start | bytes 37748740 | tf_op jit(solution)/shard_map/while
  100.1 8.3 %copy-start.1 = (f32[4,512,1536]{2,1,0:T(8,128)S(1)}, f32[4,512,1536]{2,1,0:T(8,128)}, u32[]{:S(2)}) copy-start(f32[4,512,1536]{2,1,0:T(8,128)} %get-tuple-element.201) | copy-start | bytes 37748740 | tf_op jit(solution)/shard_map/while
  125.0 8.3 %copy-start.1 = (f32[4,512,1536]{2,1,0:T(8,128)S(1)}, f32[4,512,1536]{2,1,0:T(8,128)}, u32[]{:S(2)}) copy-start(f32[4,512,1536]{2,1,0:T(8,128)} %get-tuple-element.201) | copy-start | bytes 37748740 | tf_op jit(solution)/shard_map/while
  149.8 8.3 %copy-start.1 = (f32[4,512,1536]{2,1,0:T(8,128)S(1)}, f32[4,512,1536]{2,1,0:T(8,128)}, u32[]{:S(2)}) copy-start(f32[4,512,1536]{2,1,0:T(8,128)} %get-tuple-element.201) | copy-start | bytes 37748740 | tf_op jit(solution)/shard_map/while
  174.7 8.3 %copy-start.1 = (f32[4,512,1536]{2,1,0:T(8,128)S(1)}, f32[4,512,1536]{2,1,0:T(8,128)}, u32[]{:S(2)}) copy-start(f32[4,512,1536]{2,1,0:T(8,128)} %get-tuple-element.201) | copy-start | bytes 37748740 | tf_op jit(solution)/shard_map/while
  196.8 1.8 copy-start.6
  196.8 3.5 copy-start.8
  196.8 26.3 %copy-start.2 = (bf16[1,512,768]{2,1,0:T(8,128)(2,1)S(1)}, bf16[1,512,768]{2,1,0:T(8,128)(2,1)}, u32[]{:S(2)}) copy-start(bf16[1,512,768]{2,1,0:T(8,128)(2,1)} %param.18) | copy-start | bytes 2359300
  196.8 57.7 %all-gather.6.cloned.1.call-start = ((), (), s32[]{:S(2)}) async-start(), calls=%async_computation.4 | async-start | bytes 3342336 | tf_op jit(solution)/shard_map/all_gather | solution.py:162
  197.4 93.6 %all-gather.10.cloned.1.call-start = ((), (), s32[]{:S(2)}) async-start(), calls=%async_computation.6 | async-start | bytes 3342336 | tf_op jit(solution)/shard_map/all_gather | solution.py:176
  198.0 139.2 %all-gather.8.cloned.1.call-start = ((), (), s32[]{:S(2)}) async-start(), calls=%async_computation.5 | async-start | bytes 3342336 | tf_op jit(solution)/shard_map/all_gather | solution.py:168
  232.9 4.6 %copy-start.7 = (f32[1,512,8]{1,2,0:T(8,128)S(1)}, f32[1,512,8]{1,2,0:T(8,128)}, u32[]{:S(2)}) copy-start(f32[1,512,8]{1,2,0:T(8,128)} %param.24) | copy-start | bytes 49156
  232.9 19.2 %all-to-all-start = ((bf16[4,192,768]{2,1,0:T(8,128)(2,1)}), bf16[4,192,768]{2,1,0:T(8,128)(2,1)}, u32[]{:S(2)}, u32[]{:S(2)}) async-start(bf16[4,192,768]{2,1,0:T(8,128)(2,1)} %fusion.40), calls=%async_computation.1 | async-start | bytes 2359296 | tf_op jit(solution)/shard_map/all_to_all | solution.py:156
  380.5 1.1 copy-start.3
Sparse Core Ops, SparseCore 0:
  11.9 29.8 all-gather.11
  197.0 26.0 reduce-scatter.1
Sparse Core Ops, SparseCore 1:
  199.6 45.5 all-gather.5
  247.3 43.7 all-gather.9
  293.5 43.7 all-gather.7
where the time goes:
time: 392 us; the launch traced here: 390 us
  waiting for transfers between devices  142 us (36%)
  matrix products  93.9 us (24%)
  other arithmetic  54.2 us (14%)
  local copies, waits for them, and re-layouts  43.3 us (11%)
  blocking collectives  30.4 us (8%)
  between operations  17.8 us (5%)
  starting transfers between devices  4.8 us (1%)
    all_gather x1, waiting for transfers between devices, on_device(): lax.all_gather(expert_up, 'req', axis=1, tiled=True)  46.1 us
    dot_general x5, matrix products, visit(): jnp.einsum('kqd,kjd->kqj', query, key_block, preferred_element_type=jnp.f...  40.3 us
    reduce_sum x5, other arithmetic, visit(): total = total * correction + jnp.sum(probs, -1)  34.3 us
    all_gather x1, waiting for transfers between devices, on_device(): lax.all_gather(expert_down, 'req', axis=1, tiled=True)  32.5 us
    dot_general x5, matrix products, visit(): jnp.einsum('kqj,kjd->kqd', probs.astype(jnp.bfloat16), value_block, prefe...  29.5 us
    all_to_all x1, blocking collectives, on_device(): lax.all_to_all(contrib, 'ep', split_axis=2, concat_axis=0, tiled=True)  25.2 us
    all_gather x1, waiting for transfers between devices, on_device(): rows_whole = lax.all_gather(own_rows, 'ep', axis=1, tiled=True)  25.2 us
    reduce_scatter x1, waiting for transfers between devices, on_device(): lax.psum_scatter(partial_value.astype(jnp.bfloat16), 'ep', scatter_dimens...  22.6 us
  transfers between devices with their start and end apart: 6, of which 5 were waited for; matrix products, arithmetic and copies ran while one was open for 4% of the time, Pallas kernels for 0%

commit v1 on v0

--- a/solution.py
+++ b/solution.py
@@ -4,6 +4,22 @@
 from jax.sharding import PartitionSpec as P
 
 epsilon = 1e-06
+
+
+def ring_product(x, axis, dim, term):
+    size, place, width = (lax.axis_size(axis), lax.axis_index(axis), x.shape[dim])
+    upward = [(i, (i + 1) % size) for i in range(size)]
+    left = [(i, (i - 1) % size) for i in range(size)]
+    halfway = size // 2
+    from_left = from_right = x
+    subtotal = term(x, place * width)
+    for step in range(1, halfway + 1):
+        from_left = lax.ppermute(from_left, axis, upward)
+        if step < size - halfway:
+            from_right = lax.ppermute(from_right, axis, left)
+            subtotal = subtotal + term(from_right, (place + step) % size * width)
+        subtotal = subtotal + term(from_left, (place - step) % size * width)
+    return subtotal
 
 
 def normalize(values, gain):
@@ -162,11 +178,16 @@
         lax.all_gather(expert_gate, "req", axis=1, tiled=True),
         preferred_element_type=jnp.float32,
     )
-    up_next = jnp.einsum(
-        "ecd,edf->ecf",
-        columns,
-        lax.all_gather(expert_up, "req", axis=1, tiled=True),
-        preferred_element_type=jnp.float32,
+    up_next = ring_product(
+        expert_up,
+        "req",
+        1,
+        lambda part, start_2: jnp.einsum(
+            "ecd,edf->ecf",
+            lax.dynamic_slice_in_dim(columns, start_2, part.shape[1], axis=2),
+            part,
+            preferred_element_type=jnp.float32,
+        ),
     )
     hidden_act = (jax.nn.silu(gate_next) * up_next).astype(jnp.bfloat16)
     columns = hidden_act

time: 392 us -> 349 us (0.89)
  waiting for transfers between devices: 142 us -> 48.3 us
  starting transfers between devices: 4.8 us -> 35.2 us
  matrix products: 93.9 us -> 107 us
  other arithmetic: 54.2 us -> 59.8 us
    all_gather x1 -> x0, waiting for transfers between devices: 46.1 us -> none  [on_device(): lax.all_gather(expert_up, 'req', axis=1, tiled=True)]
    ppermute x0 -> x15, starting transfers between devices: none -> 31.4 us  [the longest x7 31.4 us: ring_product(): from_right = lax.ppermute(from_right, axis, left)]
    all_gather x1, waiting for transfers between devices: 32.5 us -> 2.02 us  [on_device(): lax.all_gather(expert_down, 'req', axis=1, tiled=True)]
    reduce_scatter x1, waiting for transfers between devices: 22.6 us -> 0.01 us  [on_device(): lax.psum_scatter(partial_value.astype(jnp.bfloat16), 'ep', scatter_dimens...]
    ppermute x0 -> x15, waiting for transfers between devices: none -> 20.6 us  [the longest x7 15.5 us: ring_product(): from_right = lax.ppermute(from_right, axis, left)]
    dot_general x0 -> x15, matrix products: none -> 16.8 us  [on_device(): jnp.einsum('ecd,edf->ecf', lax.dynamic_slice_in_dim(columns, start_2, par...]
    all_to_all x1, waiting for transfers between devices: 14.2 us -> 0.01 us  [on_device(): lax.all_to_all(buffers, 'ep', split_axis=0, concat_axis=2, tiled=True)]
  transfers between devices with their start and end apart: 6 -> 20, of which waited for: 5 -> 8; matrix products, arithmetic and copies ran while one was open for 4% -> 11% of each run, Pallas kernels for 0% -> 0%
where the time goes in v1:
time: 349 us; the launch traced here: 347 us
  matrix products  107 us (31%)
  other arithmetic  59.8 us (17%)
  waiting for transfers between devices  48.3 us (14%)
  local copies, waits for them, and re-layouts  44.8 us (13%)
  starting transfers between devices  35.2 us (10%)
  blocking collectives  30.2 us (9%)
  between operations  17.9 us (5%)
    dot_general x5, matrix products, visit(): jnp.einsum('kqd,kjd->kqj', query, key_block, preferred_element_type=jnp.f...  40 us
    reduce_sum x5, other arithmetic, visit(): total = total * correction + jnp.sum(probs, -1)  34.3 us
    ppermute x7, starting transfers between devices, ring_product(): from_right = lax.ppermute(from_right, axis, left)  31.4 us
    dot_general x5, matrix products, visit(): jnp.einsum('kqj,kjd->kqd', probs.astype(jnp.bfloat16), value_block, prefe...  29.4 us
    all_to_all x1, blocking collectives, on_device(): lax.all_to_all(contrib, 'ep', split_axis=2, concat_axis=0, tiled=True)  25.2 us
    all_gather x1, waiting for transfers between devices, on_device(): rows_whole = lax.all_gather(own_rows, 'ep', axis=1, tiled=True)  25.1 us
    dot_general x15, matrix products, on_device(): jnp.einsum('ecd,edf->ecf', lax.dynamic_slice_in_dim(columns, start_2, par...  16.8 us
    ppermute x7, waiting for transfers between devices, ring_product(): from_right = lax.ppermute(from_right, axis, left)  15.5 us
  transfers between devices with their start and end apart: 20, of which 8 were waited for; matrix products, arithmetic and copies ran while one was open for 11% of the time, Pallas kernels for 0%

profile of v1, /device:TPU:0, one launch (start us, length us, event | category | flops | bytes accessed | tf_op | source)
XLA Modules:
  0.0 346.7 jit_solution(3558293803725290666)
XLA Ops:
  16.7 25.1 %all-gather.9.cloned.1.call-done = bf16[1,512,1536]{2,1,0:T(8,128)(2,1)} async-done(((bf16[1,512,768]{2,1,0:T(8,128)(2,1)}), bf16[1,512,1536]{2,1,0:T(8,128)(2,1)}) %all-gather.9.cloned.1.call-update) | async-done | bytes 1572880 | tf_op jit(solution)/shard_map/all_gather | solution.py:124
  54.8 4.0 %dynamic_update_slice.6 = bf16[4,2560,64]{1,2,0:T(8,128)(2,1)} dynamic-update-slice(bf16[4,2560,64]{1,2,0:T(8,128)(2,1)} %bitcast.133, bf16[4,512,64]{1,2,0:T(8,128)(2,1)S(1)} %pad_maximum_fusion.1, s32[]{:T(128)} %constant.145.clone.1, s32[]{:T(128)S(6)} %select_n.156, s32[]{:T(128)} %constant.145.clone.1) | dynamic-update-slice | bytes 524292 | tf_op jit(solution)/shard_map/dynamic_update_slice | solution.py:142
  61.2 3.8 %dynamic_update_slice.7 = bf16[4,2560,64]{1,2,0:T(8,128)(2,1)} dynamic-update-slice(bf16[4,2560,64]{1,2,0:T(8,128)(2,1)} %bitcast.139, bf16[4,512,64]{1,2,0:T(8,128)(2,1)S(1)} %bitcast.143, s32[]{:T(128)} %constant.145.clone.1, s32[]{:T(128)S(6)} %select_n.156, s32[]{:T(128)} %constant.145.clone.1) | dynamic-update-slice | bytes 524292 | tf_op jit(solution)/shard_map/dynamic_update_slice | solution.py:143
  65.0 123.1 %while.15 = (s32[]{:T(128)}, f32[4,1536]{1,0:T(4,128)S(1)}, f32[4,1536]{1,0:T(4,128)S(1)}, f32[4,1536,64]{1,2,0:T(8,128)}, s32[5]{0:T(128)S(1)}, /*index=5*/bf16...) while((s32[]{:T(128)}, f32[4,1536]{1,0:T(4,128)S(1)}, ...), condition=%wide.region_6.7_spmd.clone, body=%wide.region_3.6_spmd.clone.sunk | while | flops 848208896 | bytes 96092400 | solution.py:89
  67.4 8.0 %fusion.155 = (f32[4,1536]{1,0:T(4,128)S(1)}, f32[4,512,1536]{2,1,0:T(8,128)}) fusion(pred[1536,512]{0,1:T(8,128)(4,1)S(1)} %broadcast_compare_fusion.3, bf16[4,1536,64]{1,2,0:T(8,128)(2,1)} %get-tuple-element.236, bf16[4,2560,64]{1,2,0:T(8,128)(2,1)} %get-tuple-element.235, s32[]{:T(128)S(6)} %select_n.243), kind=kOutput, calls=%fused_computation.3.clone.1 | convolution fusion | flops 412084224 | bytes 14442500 | tf_op jit(solution)/shard_map/while/body/eval_jaxpr/kqd,kjd->kqj/dot_general | solution.py:67
  75.4 6.9 %fusion.156 = f32[4,1536]{1,0:T(4,128)S(1)} fusion(f32[4,512,1536]{2,1,0:T(8,128)} %get-tuple-element.201, f32[4,1536]{1,0:T(4,128)S(1)} %select_maximum_fusion.2, pred[1536,512]{0,1:T(8,128)(4,1)S(1)} %broadcast_compare_fusion.3), kind=kLoop, calls=%fused_computation.5.clone.1 | loop fusion | flops 15722496 | bytes 13418496 | tf_op jit(solution)/shard_map/while/body/eval_jaxpr/reduce_sum | solution.py:75
  83.7 5.7 %fusion.158 = f32[4,1536,64]{1,2,0:T(8,128)} fusion(f32[4,512,1536]{2,1,0:T(8,128)S(1)} %copy-done.1, f32[4,1536]{1,0:T(4,128)S(1)} %select_maximum_fusion.2, pred[1536,512]{0,1:T(8,128)(4,1)S(1)} %broadcast_compare_fusion.3, f32[4,1536,64]{1,2,0:T(8,128)} %get-tuple-element.220, f32[4,1536]{1,0:T(4,128)S(1)} %get-tuple-element.203, ...), kind=kOutput, calls=%fused_computation.8.clone.1 | convolution fusion | flops 419561472 | bytes 16826372 | tf_op jit(solution)/shard_map/while/body/eval_jaxpr/kqj,kjd->kqd/dot_general | solution.py:76
  91.8 8.0 %fusion.155 = (f32[4,1536]{1,0:T(4,128)S(1)}, f32[4,512,1536]{2,1,0:T(8,128)}) fusion(pred[1536,512]{0,1:T(8,128)(4,1)S(1)} %broadcast_compare_fusion.3, bf16[4,1536,64]{1,2,0:T(8,128)(2,1)} %get-tuple-element.236, bf16[4,2560,64]{1,2,0:T(8,128)(2,1)} %get-tuple-element.235, s32[]{:T(128)S(6)} %select_n.243), kind=kOutput, calls=%fused_computation.3.clone.1 | convolution fusion | flops 412084224 | bytes 14442500 | tf_op jit(solution)/shard_map/while/body/eval_jaxpr/kqd,kjd->kqj/dot_general | solution.py:67
  99.8 6.9 %fusion.156 = f32[4,1536]{1,0:T(4,128)S(1)} fusion(f32[4,512,1536]{2,1,0:T(8,128)} %get-tuple-element.201, f32[4,1536]{1,0:T(4,128)S(1)} %select_maximum_fusion.2, pred[1536,512]{0,1:T(8,128)(4,1)S(1)} %broadcast_compare_fusion.3), kind=kLoop, calls=%fused_computation.5.clone.1 | loop fusion | flops 15722496 | bytes 13418496 | tf_op jit(solution)/shard_map/while/body/eval_jaxpr/reduce_sum | solution.py:75
  108.1 5.9 %fusion.158 = f32[4,1536,64]{1,2,0:T(8,128)} fusion(f32[4,512,1536]{2,1,0:T(8,128)S(1)} %copy-done.1, f32[4,1536]{1,0:T(4,128)S(1)} %select_maximum_fusion.2, pred[1536,512]{0,1:T(8,128)(4,1)S(1)} %broadcast_compare_fusion.3, f32[4,1536,64]{1,2,0:T(8,128)} %get-tuple-element.220, f32[4,1536]{1,0:T(4,128)S(1)} %get-tuple-element.203, ...), kind=kOutput, calls=%fused_computation.8.clone.1 | convolution fusion | flops 419561472 | bytes 16826372 | tf_op jit(solution)/shard_map/while/body/eval_jaxpr/kqj,kjd->kqd/dot_general | solution.py:76
  116.5 8.0 %fusion.155 = (f32[4,1536]{1,0:T(4,128)S(1)}, f32[4,512,1536]{2,1,0:T(8,128)}) fusion(pred[1536,512]{0,1:T(8,128)(4,1)S(1)} %broadcast_compare_fusion.3, bf16[4,1536,64]{1,2,0:T(8,128)(2,1)} %get-tuple-element.236, bf16[4,2560,64]{1,2,0:T(8,128)(2,1)} %get-tuple-element.235, s32[]{:T(128)S(6)} %select_n.243), kind=kOutput, calls=%fused_computation.3.clone.1 | convolution fusion | flops 412084224 | bytes 14442500 | tf_op jit(solution)/shard_map/while/body/eval_jaxpr/kqd,kjd->kqj/dot_general | solution.py:67
  124.5 6.9 %fusion.156 = f32[4,1536]{1,0:T(4,128)S(1)} fusion(f32[4,512,1536]{2,1,0:T(8,128)} %get-tuple-element.201, f32[4,1536]{1,0:T(4,128)S(1)} %select_maximum_fusion.2, pred[1536,512]{0,1:T(8,128)(4,1)S(1)} %broadcast_compare_fusion.3), kind=kLoop, calls=%fused_computation.5.clone.1 | loop fusion | flops 15722496 | bytes 13418496 | tf_op jit(solution)/shard_map/while/body/eval_jaxpr/reduce_sum | solution.py:75
  132.8 5.9 %fusion.158 = f32[4,1536,64]{1,2,0:T(8,128)} fusion(f32[4,512,1536]{2,1,0:T(8,128)S(1)} %copy-done.1, f32[4,1536]{1,0:T(4,128)S(1)} %select_maximum_fusion.2, pred[1536,512]{0,1:T(8,128)(4,1)S(1)} %broadcast_compare_fusion.3, f32[4,1536,64]{1,2,0:T(8,128)} %get-tuple-element.220, f32[4,1536]{1,0:T(4,128)S(1)} %get-tuple-element.203, ...), kind=kOutput, calls=%fused_computation.8.clone.1 | convolution fusion | flops 419561472 | bytes 16826372 | tf_op jit(solution)/shard_map/while/body/eval_jaxpr/kqj,kjd->kqd/dot_general | solution.py:76
  141.2 8.0 %fusion.155 = (f32[4,1536]{1,0:T(4,128)S(1)}, f32[4,512,1536]{2,1,0:T(8,128)}) fusion(pred[1536,512]{0,1:T(8,128)(4,1)S(1)} %broadcast_compare_fusion.3, bf16[4,1536,64]{1,2,0:T(8,128)(2,1)} %get-tuple-element.236, bf16[4,2560,64]{1,2,0:T(8,128)(2,1)} %get-tuple-element.235, s32[]{:T(128)S(6)} %select_n.243), kind=kOutput, calls=%fused_computation.3.clone.1 | convolution fusion | flops 412084224 | bytes 14442500 | tf_op jit(solution)/shard_map/while/body/eval_jaxpr/kqd,kjd->kqj/dot_general | solution.py:67
  149.2 6.9 %fusion.156 = f32[4,1536]{1,0:T(4,128)S(1)} fusion(f32[4,512,1536]{2,1,0:T(8,128)} %get-tuple-element.201, f32[4,1536]{1,0:T(4,128)S(1)} %select_maximum_fusion.2, pred[1536,512]{0,1:T(8,128)(4,1)S(1)} %broadcast_compare_fusion.3), kind=kLoop, calls=%fused_computation.5.clone.1 | loop fusion | flops 15722496 | bytes 13418496 | tf_op jit(solution)/shard_map/while/body/eval_jaxpr/reduce_sum | solution.py:75
  157.4 5.9 %fusion.158 = f32[4,1536,64]{1,2,0:T(8,128)} fusion(f32[4,512,1536]{2,1,0:T(8,128)S(1)} %copy-done.1, f32[4,1536]{1,0:T(4,128)S(1)} %select_maximum_fusion.2, pred[1536,512]{0,1:T(8,128)(4,1)S(1)} %broadcast_compare_fusion.3, f32[4,1536,64]{1,2,0:T(8,128)} %get-tuple-element.220, f32[4,1536]{1,0:T(4,128)S(1)} %get-tuple-element.203, ...), kind=kOutput, calls=%fused_computation.8.clone.1 | convolution fusion | flops 419561472 | bytes 16826372 | tf_op jit(solution)/shard_map/while/body/eval_jaxpr/kqj,kjd->kqd/dot_general | solution.py:76
  165.8 8.0 %fusion.155 = (f32[4,1536]{1,0:T(4,128)S(1)}, f32[4,512,1536]{2,1,0:T(8,128)}) fusion(pred[1536,512]{0,1:T(8,128)(4,1)S(1)} %broadcast_compare_fusion.3, bf16[4,1536,64]{1,2,0:T(8,128)(2,1)} %get-tuple-element.236, bf16[4,2560,64]{1,2,0:T(8,128)(2,1)} %get-tuple-element.235, s32[]{:T(128)S(6)} %select_n.243), kind=kOutput, calls=%fused_computation.3.clone.1 | convolution fusion | flops 412084224 | bytes 14442500 | tf_op jit(solution)/shard_map/while/body/eval_jaxpr/kqd,kjd->kqj/dot_general | solution.py:67
  173.9 6.9 %fusion.156 = f32[4,1536]{1,0:T(4,128)S(1)} fusion(f32[4,512,1536]{2,1,0:T(8,128)} %get-tuple-element.201, f32[4,1536]{1,0:T(4,128)S(1)} %select_maximum_fusion.2, pred[1536,512]{0,1:T(8,128)(4,1)S(1)} %broadcast_compare_fusion.3), kind=kLoop, calls=%fused_computation.5.clone.1 | loop fusion | flops 15722496 | bytes 13418496 | tf_op jit(solution)/shard_map/while/body/eval_jaxpr/reduce_sum | solution.py:75
  182.1 5.9 %fusion.158 = f32[4,1536,64]{1,2,0:T(8,128)} fusion(f32[4,512,1536]{2,1,0:T(8,128)S(1)} %copy-done.1, f32[4,1536]{1,0:T(4,128)S(1)} %select_maximum_fusion.2, pred[1536,512]{0,1:T(8,128)(4,1)S(1)} %broadcast_compare_fusion.3, f32[4,1536,64]{1,2,0:T(8,128)} %get-tuple-element.220, f32[4,1536]{1,0:T(4,128)S(1)} %get-tuple-element.203, ...), kind=kOutput, calls=%fused_computation.8.clone.1 | convolution fusion | flops 419561472 | bytes 16826372 | tf_op jit(solution)/shard_map/while/body/eval_jaxpr/kqj,kjd->kqd/dot_general | solution.py:76
  196.9 4.4 %collective-permute-start = (bf16[2,96,512]{2,1,0:T(8,128)(2,1)S(1)}, bf16[2,96,512]{2,1,0:T(8,128)(2,1)}, u32[]{:S(2)}, u32[]{:S(2)}) collective-permute-start(bf16[2,96,512]{2,1,0:T(8,128)(2,1)S(1)} %copy-done.10), channel_id=1, source_target_pairs={{0,30},{2,0},{4,2},{6,4},{8,6},{10,8},{12,10},{14,12},{16,14},{18,... | collective-permute-start | bytes 589832 | tf_op jit(solution)/shard_map/ppermute | solution.py:19
  210.6 4.4 %collective-permute-start.2 = (bf16[2,96,512]{2,1,0:T(8,128)(2,1)}, bf16[2,96,512]{2,1,0:T(8,128)(2,1)S(1)}, u32[]{:S(2)}, u32[]{:S(2)}) collective-permute-start(bf16[2,96,512]{2,1,0:T(8,128)(2,1)} %collective-permute-done), channel_id=1, source_target_pairs={{0,30},{2,0},{4,2},{6,4},{8,6},{10,8},{12,10},{14,12},{16,14},{18,... | collective-permute-start | bytes 589832 | tf_op jit(solution)/shard_map/ppermute | solution.py:19
  219.7 4.6 %collective-permute-start.4 = (bf16[2,96,512]{2,1,0:T(8,128)(2,1)S(1)}, bf16[2,96,512]{2,1,0:T(8,128)(2,1)}, u32[]{:S(2)}, u32[]{:S(2)}) collective-permute-start(bf16[2,96,512]{2,1,0:T(8,128)(2,1)S(1)} %collective-permute-done.2), channel_id=1, source_target_pairs={{0,30},{2,0},{4,2},{6,4},{8,6},{10,8},{12,10},{14,12},{16,14},{18,... | collective-permute-start | bytes 589832 | tf_op jit(solution)/shard_map/ppermute | solution.py:19
  224.8 6.2 %collective-permute-done.4 = bf16[2,96,512]{2,1,0:T(8,128)(2,1)} collective-permute-done((bf16[2,96,512]{2,1,0:T(8,128)(2,1)S(1)}, bf16[2,96,512]{2,1,0:T(8,128)(2,1)}, u32[]{:S(2)}, u32[]{:S(2)}) %collective-permute-start.4) | collective-permute-done | bytes 196640 | tf_op jit(solution)/shard_map/ppermute | solution.py:19
  231.0 4.7 %collective-permute-start.6 = (bf16[2,96,512]{2,1,0:T(8,128)(2,1)}, bf16[2,96,512]{2,1,0:T(8,128)(2,1)}, u32[]{:S(2)}, u32[]{:S(2)}) collective-permute-start(bf16[2,96,512]{2,1,0:T(8,128)(2,1)} %collective-permute-done.4), channel_id=1, source_target_pairs={{0,30},{2,0},{4,2},{6,4},{8,6},{10,8},{12,10},{14,12},{16,14},{18,... | collective-permute-start | bytes 589832 | tf_op jit(solution)/shard_map/ppermute | solution.py:19
  237.2 4.9 %psum.7 = f32[512]{0:T(512)S(1)} all-reduce(f32[512]{0:T(512)S(1)} %fusion.28), channel_id=1, replica_groups=mesh['req'=16,'ep'=2] {'ep'}, use_global_device_ids=true, to_apply=%region_12.13 | all-reduce | flops 512 | bytes 4096 | tf_op jit(solution)/shard_map/psum | solution.py:161
  249.1 3.9 %collective-permute-start.8 = (bf16[2,96,512]{2,1,0:T(8,128)(2,1)}, bf16[2,96,512]{2,1,0:T(8,128)(2,1)}, u32[]{:S(2)}, u32[]{:S(2)}) collective-permute-start(bf16[2,96,512]{2,1,0:T(8,128)(2,1)} %collective-permute-done.6), channel_id=1, source_target_pairs={{0,30},{2,0},{4,2},{6,4},{8,6},{10,8},{12,10},{14,12},{16,14},{18,... | collective-permute-start | bytes 589832 | tf_op jit(solution)/shard_map/ppermute | solution.py:19
  256.5 4.7 %collective-permute-start.10 = (bf16[2,96,512]{2,1,0:T(8,128)(2,1)}, bf16[2,96,512]{2,1,0:T(8,128)(2,1)}, u32[]{:S(2)}, u32[]{:S(2)}) collective-permute-start(bf16[2,96,512]{2,1,0:T(8,128)(2,1)} %collective-permute-done.8), channel_id=1, source_target_pairs={{0,30},{2,0},{4,2},{6,4},{8,6},{10,8},{12,10},{14,12},{16,14},{18,... | collective-permute-start | bytes 589832 | tf_op jit(solution)/shard_map/ppermute | solution.py:19
  262.3 3.9 %collective-permute-done.10 = bf16[2,96,512]{2,1,0:T(8,128)(2,1)} collective-permute-done((bf16[2,96,512]{2,1,0:T(8,128)(2,1)}, bf16[2,96,512]{2,1,0:T(8,128)(2,1)}, u32[]{:S(2)}, u32[]{:S(2)}) %collective-permute-start.10) | collective-permute-done | bytes 196640 | tf_op jit(solution)/shard_map/ppermute | solution.py:19
  266.2 4.6 %collective-permute-start.12 = (bf16[2,96,512]{2,1,0:T(8,128)(2,1)}, bf16[2,96,512]{2,1,0:T(8,128)(2,1)}, u32[]{:S(2)}, u32[]{:S(2)}) collective-permute-start(bf16[2,96,512]{2,1,0:T(8,128)(2,1)} %collective-permute-done.10), channel_id=1, source_target_pairs={{0,30},{2,0},{4,2},{6,4},{8,6},{10,8},{12,10},{14,12},{16,14},{18,... | collective-permute-start | bytes 589832 | tf_op jit(solution)/shard_map/ppermute | solution.py:19
  297.5 4.5 %fusion.27 = bf16[2,192,1536]{2,1,0:T(8,128)(2,1)} fusion(bf16[2,512,1536]{2,1,0:T(8,128)(2,1)} %all-gather.7.cloned.1.call-done, f32[2,192,512]{2,1,0:T(8,128)} %fusion.44, bf16[2,96,512]{2,1,0:T(8,128)(2,1)} %collective-permute-done.14, f32[2,192]{1,0:T(2,128)S(1)} %constant_dynamic-slice_fusion, f32[2,192,512]{2,1,0:T(8,128)} %fusion.116, ...), kind=kOutput, calls=%fused_computation.39 | convolution fusion | flops 644284416 | bytes 6195204 | tf_op jit(solution)/shard_map/ecf,efd->ecd/dot_general | solution.py:194
  302.0 4.8 %copy.57 = bf16[2,192,1536]{1,0,2:T(2,128)(2,1)} copy(bf16[2,192,1536]{2,1,0:T(8,128)(2,1)} %fusion.27) | data formatting | bytes 2359296 | tf_op jit(solution)/shard_map/convert_element_type | solution.py:200
  306.9 25.2 %all_to_all.36 = bf16[2,192,1536]{1,0,2:T(2,128)(2,1)} all-to-all(bf16[2,192,1536]{1,0,2:T(2,128)(2,1)} %copy.57), channel_id=1, replica_groups=mesh['req'=16,'ep'=2] {'ep'}, dimensions={2} | all-to-all | bytes 2359296 | tf_op jit(solution)/shard_map/all_to_all | solution.py:201
  (187 shorter events, 107.8 us)
Async XLA Ops:
  8.0 185.4 %copy-start = (bf16[768,1536]{1,0:T(8,128)(2,1)S(1)}, bf16[768,1536]{1,0:T(8,128)(2,1)}, u32[]{:S(2)}) copy-start(bf16[768,1536]{1,0:T(8,128)(2,1)} %param.30) | copy-start | bytes 7077892
  8.0 33.8 %all-gather.9.cloned.1.call-start = ((), (), s32[]{:S(2)}) async-start(), calls=%async_computation.6 | async-start | bytes 2359296 | tf_op jit(solution)/shard_map/all_gather | solution.py:124
  11.8 32.0 %copy-start.19 = (f32[1536]{0:T(1024)S(1)}, f32[1536]{0:T(1024)}, u32[]{:S(2)}) copy-start(f32[1536]{0:T(1024)} %param.25) | copy-start | bytes 18436
  11.8 224.0 %reduce-scatter.2.cloned.1.call-start = ((), (), s32[]{:S(2)}) async-start(), calls=%async_computation.3 | async-start | bytes 2359296 | tf_op jit(solution)/shard_map/reduce_scatter | solution.py:152
  75.4 8.3 %copy-start.1 = (f32[4,512,1536]{2,1,0:T(8,128)S(1)}, f32[4,512,1536]{2,1,0:T(8,128)}, u32[]{:S(2)}) copy-start(f32[4,512,1536]{2,1,0:T(8,128)} %get-tuple-element.201) | copy-start | bytes 37748740 | tf_op jit(solution)/shard_map/while
  99.8 8.3 %copy-start.1 = (f32[4,512,1536]{2,1,0:T(8,128)S(1)}, f32[4,512,1536]{2,1,0:T(8,128)}, u32[]{:S(2)}) copy-start(f32[4,512,1536]{2,1,0:T(8,128)} %get-tuple-element.201) | copy-start | bytes 37748740 | tf_op jit(solution)/shard_map/while
  124.5 8.3 %copy-start.1 = (f32[4,512,1536]{2,1,0:T(8,128)S(1)}, f32[4,512,1536]{2,1,0:T(8,128)}, u32[]{:S(2)}) copy-start(f32[4,512,1536]{2,1,0:T(8,128)} %get-tuple-element.201) | copy-start | bytes 37748740 | tf_op jit(solution)/shard_map/while
  149.2 8.3 %copy-start.1 = (f32[4,512,1536]{2,1,0:T(8,128)S(1)}, f32[4,512,1536]{2,1,0:T(8,128)}, u32[]{:S(2)}) copy-start(f32[4,512,1536]{2,1,0:T(8,128)} %get-tuple-element.201) | copy-start | bytes 37748740 | tf_op jit(solution)/shard_map/while
  173.8 8.3 %copy-start.1 = (f32[4,512,1536]{2,1,0:T(8,128)S(1)}, f32[4,512,1536]{2,1,0:T(8,128)}, u32[]{:S(2)}) copy-start(f32[4,512,1536]{2,1,0:T(8,128)} %get-tuple-element.201) | copy-start | bytes 37748740 | tf_op jit(solution)/shard_map/while
  196.0 39.8 %copy-start.2 = (bf16[1,512,768]{2,1,0:T(8,128)(2,1)S(1)}, bf16[1,512,768]{2,1,0:T(8,128)(2,1)}, u32[]{:S(2)}) copy-start(bf16[1,512,768]{2,1,0:T(8,128)(2,1)} %param.18) | copy-start | bytes 2359300
  196.0 96.0 %all-gather.5.cloned.1.call-start = ((), (), s32[]{:S(2)}) async-start(), calls=%async_computation.4 | async-start | bytes 3342336 | tf_op jit(solution)/shard_map/all_gather | solution.py:178
  196.6 101.0 %all-gather.7.cloned.1.call-start = ((), (), s32[]{:S(2)}) async-start(), calls=%async_computation.5 | async-start | bytes 3342336 | tf_op jit(solution)/shard_map/all_gather | solution.py:197
  196.9 7.9 %collective-permute-start.1 = (bf16[2,96,512]{2,1,0:T(8,128)(2,1)S(1)}, bf16[2,96,512]{2,1,0:T(8,128)(2,1)S(1)}, u32[]{:S(2)}, u32[]{:S(2)}) collective-permute-start(bf16[2,96,512]{2,1,0:T(8,128)(2,1)S(1)} %copy-done.10), channel_id=1, source_target_pairs={{0,2},{2,4},{4,6},{6,8},{8,10},{10,12},{12,14},{14,16},{16,18},{18... | collective-permute-start | bytes 589832 | tf_op jit(solution)/shard_map/ppermute | solution.py:17
  196.9 13.7 %collective-permute-start = (bf16[2,96,512]{2,1,0:T(8,128)(2,1)S(1)}, bf16[2,96,512]{2,1,0:T(8,128)(2,1)}, u32[]{:S(2)}, u32[]{:S(2)}) collective-permute-start(bf16[2,96,512]{2,1,0:T(8,128)(2,1)S(1)} %copy-done.10), channel_id=1, source_target_pairs={{0,30},{2,0},{4,2},{6,4},{8,6},{10,8},{12,10},{14,12},{16,14},{18,... | collective-permute-start | bytes 589832 | tf_op jit(solution)/shard_map/ppermute | solution.py:19
  204.8 40.7 %copy-start.12 = (bf16[2,96,512]{2,1,0:T(8,128)(2,1)}, bf16[2,96,512]{2,1,0:T(8,128)(2,1)S(1)}, u32[]{:S(2)}) copy-start(bf16[2,96,512]{2,1,0:T(8,128)(2,1)S(1)} %collective-permute-done.1) | copy-start | bytes 589828
  204.8 10.2 %collective-permute-start.3 = (bf16[2,96,512]{2,1,0:T(8,128)(2,1)S(1)}, bf16[2,96,512]{2,1,0:T(8,128)(2,1)}, u32[]{:S(2)}, u32[]{:S(2)}) collective-permute-start(bf16[2,96,512]{2,1,0:T(8,128)(2,1)S(1)} %collective-permute-done.1), channel_id=1, source_target_pairs={{0,2},{2,4},{4,6},{6,8},{8,10},{10,12},{12,14},{14,16},{16,18},{18... | collective-permute-start | bytes 589832 | tf_op jit(solution)/shard_map/ppermute | solution.py:17
  210.6 9.1 %collective-permute-start.2 = (bf16[2,96,512]{2,1,0:T(8,128)(2,1)}, bf16[2,96,512]{2,1,0:T(8,128)(2,1)S(1)}, u32[]{:S(2)}, u32[]{:S(2)}) collective-permute-start(bf16[2,96,512]{2,1,0:T(8,128)(2,1)} %collective-permute-done), channel_id=1, source_target_pairs={{0,30},{2,0},{4,2},{6,4},{8,6},{10,8},{12,10},{14,12},{16,14},{18,... | collective-permute-start | bytes 589832 | tf_op jit(solution)/shard_map/ppermute | solution.py:19
  215.0 9.3 %collective-permute-start.5 = (bf16[2,96,512]{2,1,0:T(8,128)(2,1)}, bf16[2,96,512]{2,1,0:T(8,128)(2,1)}, u32[]{:S(2)}, u32[]{:S(2)}) collective-permute-start(bf16[2,96,512]{2,1,0:T(8,128)(2,1)} %collective-permute-done.3), channel_id=1, source_target_pairs={{0,2},{2,4},{4,6},{6,8},{8,10},{10,12},{12,14},{14,16},{16,18},{18... | collective-permute-start | bytes 589832 | tf_op jit(solution)/shard_map/ppermute | solution.py:17
  215.7 26.5 %copy-start.15 = (s32[1,4,4,128]{3,1,2,0:T(4,128)}, s32[1,4,4,128]{3,1,2,0:T(4,128)S(1)}, u32[]{:S(2)}) copy-start(s32[1,4,4,128]{3,1,2,0:T(4,128)S(1)} %copy.64) | copy-start | bytes 24580
  219.7 25.8 %copy-start.8 = (bf16[2,96,512]{2,1,0:T(8,128)(2,1)}, bf16[2,96,512]{2,1,0:T(8,128)(2,1)S(1)}, u32[]{:S(2)}) copy-start(bf16[2,96,512]{2,1,0:T(8,128)(2,1)S(1)} %collective-permute-done.2) | copy-start | bytes 589828
  219.7 11.4 %collective-permute-start.4 = (bf16[2,96,512]{2,1,0:T(8,128)(2,1)S(1)}, bf16[2,96,512]{2,1,0:T(8,128)(2,1)}, u32[]{:S(2)}, u32[]{:S(2)}) collective-permute-start(bf16[2,96,512]{2,1,0:T(8,128)(2,1)S(1)} %collective-permute-done.2), channel_id=1, source_target_pairs={{0,30},{2,0},{4,2},{6,4},{8,6},{10,8},{12,10},{14,12},{16,14},{18,... | collective-permute-start | bytes 589832 | tf_op jit(solution)/shard_map/ppermute | solution.py:19
  224.3 11.5 %collective-permute-start.7 = (bf16[2,96,512]{2,1,0:T(8,128)(2,1)}, bf16[2,96,512]{2,1,0:T(8,128)(2,1)}, u32[]{:S(2)}, u32[]{:S(2)}) collective-permute-start(bf16[2,96,512]{2,1,0:T(8,128)(2,1)} %collective-permute-done.5), channel_id=1, source_target_pairs={{0,2},{2,4},{4,6},{6,8},{8,10},{10,12},{12,14},{14,16},{16,18},{18... | collective-permute-start | bytes 589832 | tf_op jit(solution)/shard_map/ppermute | solution.py:17
  231.0 18.0 %collective-permute-start.6 = (bf16[2,96,512]{2,1,0:T(8,128)(2,1)}, bf16[2,96,512]{2,1,0:T(8,128)(2,1)}, u32[]{:S(2)}, u32[]{:S(2)}) collective-permute-start(bf16[2,96,512]{2,1,0:T(8,128)(2,1)} %collective-permute-done.4), channel_id=1, source_target_pairs={{0,30},{2,0},{4,2},{6,4},{8,6},{10,8},{12,10},{14,12},{16,14},{18,... | collective-permute-start | bytes 589832 | tf_op jit(solution)/shard_map/ppermute | solution.py:19
  235.8 17.2 %collective-permute-start.9 = (bf16[2,96,512]{2,1,0:T(8,128)(2,1)}, bf16[2,96,512]{2,1,0:T(8,128)(2,1)}, u32[]{:S(2)}, u32[]{:S(2)}) collective-permute-start(bf16[2,96,512]{2,1,0:T(8,128)(2,1)} %collective-permute-done.7), channel_id=1, source_target_pairs={{0,2},{2,4},{4,6},{6,8},{8,10},{10,12},{12,14},{14,16},{16,18},{18... | collective-permute-start | bytes 589832 | tf_op jit(solution)/shard_map/ppermute | solution.py:17
  245.5 7.5 %copy-start.14 = (s32[1,512,8]{1,2,0:T(8,128)S(1)}, s32[1,512,8]{1,2,0:T(8,128)}, u32[]{:S(2)}) copy-start(s32[1,512,8]{1,2,0:T(8,128)} %param.23) | copy-start | bytes 49156
  245.5 27.1 %all-to-all-start = ((bf16[4,192,768]{2,1,0:T(8,128)(2,1)}), bf16[4,192,768]{2,1,0:T(8,128)(2,1)S(1)}, u32[]{:S(2)}, u32[]{:S(2)}) async-start(bf16[4,192,768]{2,1,0:T(8,128)(2,1)} %fusion.40), calls=%async_computation.1 | async-start | bytes 2359296 | tf_op jit(solution)/shard_map/all_to_all | solution.py:172
  249.1 7.4 %collective-permute-start.8 = (bf16[2,96,512]{2,1,0:T(8,128)(2,1)}, bf16[2,96,512]{2,1,0:T(8,128)(2,1)}, u32[]{:S(2)}, u32[]{:S(2)}) collective-permute-start(bf16[2,96,512]{2,1,0:T(8,128)(2,1)} %collective-permute-done.6), channel_id=1, source_target_pairs={{0,30},{2,0},{4,2},{6,4},{8,6},{10,8},{12,10},{14,12},{16,14},{18,... | collective-permute-start | bytes 589832 | tf_op jit(solution)/shard_map/ppermute | solution.py:19
  253.0 8.2 %collective-permute-start.11 = (bf16[2,96,512]{2,1,0:T(8,128)(2,1)}, bf16[2,96,512]{2,1,0:T(8,128)(2,1)}, u32[]{:S(2)}, u32[]{:S(2)}) collective-permute-start(bf16[2,96,512]{2,1,0:T(8,128)(2,1)} %collective-permute-done.9), channel_id=1, source_target_pairs={{0,2},{2,4},{4,6},{6,8},{8,10},{10,12},{12,14},{14,16},{16,18},{18... | collective-permute-start | bytes 589832 | tf_op jit(solution)/shard_map/ppermute | solution.py:17
  256.5 9.8 %collective-permute-start.10 = (bf16[2,96,512]{2,1,0:T(8,128)(2,1)}, bf16[2,96,512]{2,1,0:T(8,128)(2,1)}, u32[]{:S(2)}, u32[]{:S(2)}) collective-permute-start(bf16[2,96,512]{2,1,0:T(8,128)(2,1)} %collective-permute-done.8), channel_id=1, source_target_pairs={{0,30},{2,0},{4,2},{6,4},{8,6},{10,8},{12,10},{14,12},{16,14},{18,... | collective-permute-start | bytes 589832 | tf_op jit(solution)/shard_map/ppermute | solution.py:19
  261.2 11.4 %collective-permute-start.13 = (bf16[2,96,512]{2,1,0:T(8,128)(2,1)}, bf16[2,96,512]{2,1,0:T(8,128)(2,1)}, u32[]{:S(2)}, u32[]{:S(2)}) collective-permute-start(bf16[2,96,512]{2,1,0:T(8,128)(2,1)} %collective-permute-done.11), channel_id=1, source_target_pairs={{0,2},{2,4},{4,6},{6,8},{8,10},{10,12},{12,14},{14,16},{16,18},{18... | collective-permute-start | bytes 589832 | tf_op jit(solution)/shard_map/ppermute | solution.py:17
  266.2 23.6 %collective-permute-start.12 = (bf16[2,96,512]{2,1,0:T(8,128)(2,1)}, bf16[2,96,512]{2,1,0:T(8,128)(2,1)}, u32[]{:S(2)}, u32[]{:S(2)}) collective-permute-start(bf16[2,96,512]{2,1,0:T(8,128)(2,1)} %collective-permute-done.10), channel_id=1, source_target_pairs={{0,30},{2,0},{4,2},{6,4},{8,6},{10,8},{12,10},{14,12},{16,14},{18,... | collective-permute-start | bytes 589832 | tf_op jit(solution)/shard_map/ppermute | solution.py:19
  272.5 23.0 %collective-permute-start.14 = (bf16[2,96,512]{2,1,0:T(8,128)(2,1)}, bf16[2,96,512]{2,1,0:T(8,128)(2,1)}, u32[]{:S(2)}, u32[]{:S(2)}) collective-permute-start(bf16[2,96,512]{2,1,0:T(8,128)(2,1)} %collective-permute-done.13), channel_id=1, source_target_pairs={{0,2},{2,4},{4,6},{6,8},{8,10},{10,12},{12,14},{14,16},{16,18},{18... | collective-permute-start | bytes 589832 | tf_op jit(solution)/shard_map/ppermute | solution.py:17
  (14 other events, 27.0 us)
Sparse Core Ops, SparseCore 0:
  11.9 29.8 all-gather.8
  196.1 26.0 reduce-scatter.1
Sparse Core Ops, SparseCore 1:
  198.7 50.4 all-gather.4
  251.3 46.2 all-gather.6
